TPU v7x, 128 devices: a whole 4x4x4 slice. The times are simulated.
128 devices in a mesh: view: 4 (over y), block: 32 (over z, x, core).
Axes of the slice: x: 4, y: 4, z: 4, core: 2. Of those that a mesh axis runs over, the one named last changes fastest.
Arguments:
- estimate: float32 [512, 128, 256], P('block'), may hold values from 0.3 to 3
- observed: float32 [4, 512, 2, 128, 256], P('view', 'block'), may hold values from 0.2 to 5
- route_dest: int32 [4, 512], P('view', 'block'), may hold values from -1 to 31, as said below
- route_pos: int32 [4, 512], P('view', 'block'), may hold values from -1 to 15, as said below
- view_span: int32 [8, 2], P('view'), may hold values from 0 to 256, as said below
- view_count: int32 [256], P('block'), may hold values from 4 to 8, as said below
- psf_taps: float32 [8, 3, 31], P('view'), may hold values from 0 to 2, as said below
- view_weight: float32 [8], P('view'), may hold values from 1 to 4
Outputs:
- restored: float32 [512, 128, 256], P('block')
Inputs may be any that keep to these rules, and one draw needn't show every extreme that they name: `route_dest`: in each view group, every brick of one of its views that lies inside that view's sub-volume stands in exactly one slot of the group's devices, with its owner block and position (view of the group times 8 plus brick of the block); other slots hold -1. One device's slots send at most 1 bricks to one block, and some device sends 1 to some block. `route_pos`: position of the slot's brick as described for route_dest, -1 together with it. `view_span`: each sub-volume lies within the 256 bricks and holds at least 128 of them; the first view of each view group spans all of them. `view_count`: equals the number of views whose span holds the brick. `psf_taps`: each kernel is positive.
All inputs are finite; a program needn't handle non-finite values.
Results may differ from a plain program's by a relative error of at most 0.0003.
Values sent between devices are 32-bit elements; how exact they have to be, the bound alone decides.
No kernel may reach another device: no remote copies, remote signals or barrier semaphores. Data moves between devices by JAX's collectives and lax.ppermute only.
A program may use at most 128 MiB of HBM per device.

v0:
```python
import jax
import jax.numpy as jnp
from jax import lax
from jax.sharding import PartitionSpec as P

ITERS = 2


def with_halo(cells, sides, width):
    for axis, dim in sides:
        count = lax.axis_size(axis)
        ends = count - 1
        head = lax.slice_in_dim(cells, 0, width, axis=dim)
        tail = lax.slice_in_dim(cells, cells.shape[dim] - width, cells.shape[dim], axis=dim)
        cells = jnp.concatenate(
            [
                lax.ppermute(tail, axis, [(i, (i + 1) % count) for i in range(ends)]),
                cells,
                lax.ppermute(head, axis, [((i + 1) % count, i) for i in range(ends)]),
            ],
            axis=dim,
        )
    return cells


def banded_blur_matrix(filter_tap_values, row_count, col_count, offset_base, orientation):
    tap_count = filter_tap_values.shape[-1]
    grid_shape = (row_count, col_count, tap_count)
    row_index = lax.broadcasted_iota(jnp.int32, grid_shape, 0)
    col_index = lax.broadcasted_iota(jnp.int32, grid_shape, 1)
    tap_index = lax.broadcasted_iota(jnp.int32, grid_shape, 2)
    selected_entries = (orientation * (row_index - col_index) + offset_base == tap_index).astype(
        jnp.float32
    )
    return jnp.einsum(
        "ewq,gq->gew", selected_entries, filter_tap_values, precision=lax.Precision.HIGHEST
    )


def on_device(
    estimate, observed, route_dest, route_pos, view_span, view_count, psf_taps, view_weight
):
    highest = lax.Precision.HIGHEST
    blocks = lax.axis_size("block")
    slot_count = observed.shape[1]
    planes = observed.shape[2]
    ny_cells = observed.shape[3]
    nz_cells = observed.shape[4]
    per_group = view_span.shape[0]
    per_block = view_count.shape[0]
    capacity = max(1, slot_count // blocks)
    block_x = per_block * planes
    reach = psf_taps.shape[-1] // 2
    sources = observed[0]
    dest_list = route_dest[0]
    pos_list = route_pos[0]
    slot_index = jnp.arange(slot_count, dtype=jnp.int32)
    earlier = (dest_list[:, None] == dest_list[None, :]) & (
        slot_index[None, :] < slot_index[:, None]
    )
    rank_in_dest = jnp.sum(earlier.astype(jnp.int32), axis=1)
    target = jnp.where(dest_list >= 0, dest_list * capacity + rank_in_dest, blocks * capacity)
    outgoing = (
        jnp.zeros((blocks * capacity, planes, ny_cells, nz_cells), jnp.float32)
        .at[target]
        .set(sources, mode="drop")
    )
    out_pos = (
        jnp.full((blocks * capacity,), -1.0, jnp.float32)
        .at[target]
        .set(pos_list.astype(jnp.float32), mode="drop")
    )
    arrived, arrived_pos = (
        lax.all_to_all(
            outgoing.reshape(blocks, capacity, planes, ny_cells, nz_cells),
            "block",
            split_axis=0,
            concat_axis=0,
            tiled=True,
        ),
        lax.all_to_all(
            out_pos.reshape(blocks, capacity), "block", split_axis=0, concat_axis=0, tiled=True
        ),
    )
    places = arrived_pos.reshape(-1).astype(jnp.int32)
    places = jnp.where(places >= 0, places, per_group * per_block)
    placed = (
        jnp.zeros((per_group * per_block, planes, ny_cells, nz_cells), jnp.float32)
        .at[places]
        .set(arrived.reshape(-1, planes, ny_cells, nz_cells), mode="drop")
    )
    obs_views = placed.reshape(per_group, block_x, ny_cells, nz_cells)
    brick_index = lax.axis_index("block") * per_block + jnp.arange(per_block, dtype=jnp.int32)
    span_first = view_span[:, 0:1]
    span_length = view_span[:, 1:2]
    inside = (
        (brick_index[None, :] >= span_first) & (brick_index[None, :] < span_first + span_length)
    ).astype(jnp.float32)
    live_cells = jnp.repeat(inside, planes, axis=1)[:, :, None, None]
    counts = jnp.repeat(view_count.astype(jnp.float32), planes)[:, None, None]
    point_spread_kernels = psf_taps / jnp.sum(psf_taps, axis=-1, keepdims=True)
    fwd_x = banded_blur_matrix(point_spread_kernels[:, 0], block_x + 2 * reach, block_x, 0, 1)
    adj_x = banded_blur_matrix(
        point_spread_kernels[:, 0], block_x + 2 * reach, block_x, 2 * reach, -1
    )
    mat_y = banded_blur_matrix(point_spread_kernels[:, 1], ny_cells, ny_cells, reach, 1)
    mat_z = banded_blur_matrix(point_spread_kernels[:, 2], nz_cells, nz_cells, reach, 1)
    weights = view_weight[:, None, None, None]
    current = estimate
    for iteration in range(ITERS):
        padded = with_halo(current, (("block", 0),), reach)
        along_x = jnp.einsum("wyz,vwx->vxyz", padded, fwd_x, precision=highest)
        lateral_y_pass = jnp.einsum("vxyz,vyq->vxqz", along_x, mat_y, precision=highest)
        blurred = jnp.einsum("vxyz,vzq->vxyq", lateral_y_pass, mat_z, precision=highest)
        ratios = live_cells * (obs_views / blurred) + (1.0 - live_cells)
        back_z = jnp.einsum("vxyz,vqz->vxyq", ratios, mat_z, precision=highest)
        back_y = jnp.einsum("vxyz,vqy->vxqz", back_z, mat_y, precision=highest)
        rimmed = with_halo(back_y, (("block", 1),), reach)
        corrected = jnp.einsum("vwyz,vwx->vxyz", rimmed, adj_x, precision=highest)
        partial_logarithm = jnp.sum(live_cells * weights * jnp.log(corrected), axis=0)
        summed = lax.psum(partial_logarithm, "view")
        current = current * jnp.exp(summed / counts)
    return current


def solution(mesh):
    placed = (
        P("block", None, None),
        P("view", "block", None, None, None),
        P("view", "block"),
        P("view", "block"),
        P("view", None),
        P("block"),
        P("view", None, None),
        P("view"),
    )
    return jax.shard_map(
        on_device, mesh=mesh, in_specs=placed, out_specs=P("block", None, None), check_vma=False
    )
```

profile of v0, /device:TPU:1, one launch (start us, length us, event | category | flops | bytes accessed | tf_op | source)
XLA Modules:
  0.0 547.7 jit_solution(2459085685893780492)
XLA Ops:
  10.1 9.4 %all-to-all-start = ((f32[32,1,1]{2,1,0:T(1,128)}), f32[32,1,1]{2,1,0:T(1,128)S(1)}, u32[]{:S(2)}, u32[]{:S(2)}) async-start(f32[32,1,1]{2,1,0:T(1,128)} %copy.91), calls=%async_computation | async-start | bytes 32768 | tf_op jit(solution)/shard_map/all_to_all | solution.py:81
  19.5 4.2 broadcast_in_dim.37
  23.8 7.5 %scatter_fusion = f32[32,2,128,256]{3,2,1,0:T(8,128)} fusion(f32[32,2,128,256]{3,2,1,0:T(8,128)} %broadcast_in_dim.37, s32[16]{0:T(128)S(1)} %fusion.58, f32[16,2,128,256]{3,2,1,0:T(8,128)} %bitcast.92), kind=kCustom, calls=%fused_computation.1 | custom fusion | bytes 12582976 | tf_op jit(solution)/shard_map/scatter | solution.py:66
  31.2 8.0 %all-to-all-start.1 = ((f32[32,1,2,128,256]{4,3,2,1,0:T(8,128)}), f32[32,1,2,128,256]{4,3,2,1,0:T(8,128)}, u32[]{:S(2)}, u32[]{:S(2)}) async-start(f32[32,1,2,128,256]{4,3,2,1,0:T(8,128)} %bitcast.89), calls=%async_computation.1 | async-start | bytes 16777216 | tf_op jit(solution)/shard_map/all_to_all | solution.py:74
  54.9 100.3 %collective-permute-done = f32[15,128,256]{2,1,0:T(8,128)} collective-permute-done((f32[15,128,256]{2,1,0:T(8,128)}, f32[15,128,256]{2,1,0:T(8,128)}, u32[]{:S(2)}, u32[]{:S(2)}) %collective-permute-start) | collective-permute-done | bytes 1966112 | tf_op jit(solution)/shard_map/ppermute | solution.py:17
  162.4 4.7 fusion.5
  167.1 17.1 %fusion.29 = f32[2,128,16,256]{3,1,2,0:T(8,128)S(1)} fusion(f32[2,128,128,1]{1,2,3,0:T(8,128)S(1)} %copy.118, f32[2,16,128,256]{3,1,2,0:T(8,128)S(1)} %fusion.5), kind=kOutput, calls=%fused_computation.37 | convolution fusion | flops 1610612736 | bytes 8519680 | tf_op jit(solution)/shard_map/vxyz,vyq->vxqz/dot_general | solution.py:113
  184.2 4.9 fusion.17
  191.6 13.0 %scatter_fusion.1 = f32[16,2,128,256]{3,2,1,0:T(8,128)} fusion(f32[16,2,128,256]{3,2,1,0:T(8,128)} %broadcast_in_dim.33, s32[32]{0:T(128)S(1)} %fusion.57, f32[32,2,128,256]{3,2,1,0:T(8,128)} %bitcast.15), kind=kCustom, calls=%fused_computation.2 | custom fusion | bytes 25165952 | tf_op jit(solution)/shard_map/scatter | solution.py:90
  204.6 6.4 %fusion.21 = f32[2,16,128,256]{3,2,1,0:T(8,128)S(1)} fusion(f32[2,16,128,256]{3,2,1,0:T(8,128)} %fusion.17, f32[2,16]{1,0:T(2,128)S(1)} %get-tuple-element.16, f32[2,16]{1,0:T(2,128)S(1)} %broadcast_in_dim_reshape.4, f32[2,256,256,1]{2,0,1,3:T(2,128)S(1)} %fusion.41, f32[2,16,128,256]{3,2,1,0:T(8,128)} %bitcast.90), kind=kOutput, calls=%fused_computation.31 | convolution fusion | flops 3224371200 | bytes 13107456 | tf_op jit(solution)/shard_map/vxyz,vqz->vxyq/dot_general | solution.py:116
  220.5 39.8 %collective-permute-done.2 = f32[2,15,128,256]{3,2,1,0:T(8,128)S(1)} collective-permute-done((f32[2,15,128,256]{3,2,1,0:T(8,128)S(1)}, f32[2,15,128,256]{3,2,1,0:T(8,128)S(1)}, u32[]{:S(2)}, u32[]{:S(2)}) %collective-permute-start.2) | collective-permute-done | bytes 3932192 | tf_op jit(solution)/shard_map/ppermute | solution.py:17
  260.4 4.4 collective-permute-done.3
  267.5 13.2 %multiply_reduce_fusion.1 = f32[16,128,256]{2,0,1:T(8,128)} fusion(f32[2,46,128,256]{3,2,1,0:T(8,128)S(1)} %pad_maximum_fusion, f32[2,16]{1,0:T(2,128)S(1)} %get-tuple-element.15, f32[2,46,16,1]{1,0,2,3:T(2,128)S(1)} %convolution_bitcast_fusion.3), kind=kOutput, calls=%fused_computation.40 | convolution fusion | flops 580386816 | bytes 14161792 | tf_op jit(solution)/shard_map/vwyz,vwx->vxyz/dot_general | solution.py:119
  280.9 67.0 %all-reduce.3.cloned.1.call-done = f32[16,128,256]{2,0,1:T(8,128)} async-done(((f32[16,128,256]{2,0,1:T(8,128)}), f32[16,128,256]{2,0,1:T(8,128)}) %all-reduce.3.cloned.1.call-update) | async-done | bytes 2097168 | tf_op jit(solution)/shard_map/psum | solution.py:121
  360.3 18.3 %collective-permute-done.4 = f32[15,128,256]{2,1,0:T(8,128)S(1)} collective-permute-done((f32[15,128,256]{2,1,0:T(8,128)S(1)}, f32[15,128,256]{2,1,0:T(8,128)S(1)}, u32[]{:S(2)}, u32[]{:S(2)}) %collective-permute-start.4) | collective-permute-done | bytes 1966112 | tf_op jit(solution)/shard_map/ppermute | solution.py:17
  379.7 4.4 collective-permute-done.5
  385.3 4.7 fusion.10
  390.0 6.3 %fusion.27 = f32[2,128,16,256]{3,1,2,0:T(8,128)S(1)} fusion(f32[2,128,128,1]{1,2,3,0:T(8,128)S(1)} %copy.118, f32[2,16,128,256]{3,1,2,0:T(8,128)S(1)} %fusion.10), kind=kOutput, calls=%fused_computation.35 | convolution fusion | flops 1610612736 | bytes 8519680 | tf_op jit(solution)/shard_map/vxyz,vyq->vxqz/dot_general | solution.py:113
  400.0 4.4 fusion.25
  404.4 4.0 convolution_bitcast_fusion
  414.0 40.0 %collective-permute-done.6 = f32[2,15,128,256]{3,2,1,0:T(8,128)S(1)} collective-permute-done((f32[2,15,128,256]{3,2,1,0:T(8,128)S(1)}, f32[2,15,128,256]{3,2,1,0:T(8,128)S(1)}, u32[]{:S(2)}, u32[]{:S(2)}) %collective-permute-start.6) | collective-permute-done | bytes 3932192 | tf_op jit(solution)/shard_map/ppermute | solution.py:17
  454.0 4.4 collective-permute-done.7
  460.8 13.2 %multiply_reduce_fusion = f32[16,128,256]{2,0,1:T(8,128)} fusion(f32[2,46,128,256]{3,2,1,0:T(8,128)S(1)} %pad_maximum_fusion.1, f32[2,16]{1,0:T(2,128)S(1)} %get-tuple-element.15, f32[2,46,16,1]{1,0,2,3:T(2,128)S(1)} %convolution_bitcast_fusion.3), kind=kOutput, calls=%fused_computation.39 | convolution fusion | flops 580386816 | bytes 14161792 | tf_op jit(solution)/shard_map/vwyz,vwx->vxyz/dot_general | solution.py:119
  474.1 61.6 %all-reduce.5.cloned.1.call-done = f32[16,128,256]{2,0,1:T(8,128)} async-done(((f32[16,128,256]{2,0,1:T(8,128)}), f32[16,128,256]{2,0,1:T(8,128)}) %all-reduce.5.cloned.1.call-update) | async-done | bytes 2097168 | tf_op jit(solution)/shard_map/psum | solution.py:121
  (71 shorter events, 72.0 us)
Async XLA Ops:
  10.1 21.1 %all-to-all-start = ((f32[32,1,1]{2,1,0:T(1,128)}), f32[32,1,1]{2,1,0:T(1,128)S(1)}, u32[]{:S(2)}, u32[]{:S(2)}) async-start(f32[32,1,1]{2,1,0:T(1,128)} %copy.91), calls=%async_computation | async-start | bytes 32768 | tf_op jit(solution)/shard_map/all_to_all | solution.py:81
  31.2 8.1 %copy-start.1 = (f32[16,128,256]{2,1,0:T(8,128)S(1)}, f32[16,128,256]{2,1,0:T(8,128)}, u32[]{:S(2)}) copy-start(f32[16,128,256]{2,1,0:T(8,128)} %param.8) | copy-start | bytes 6291460
  31.2 157.9 %all-to-all-start.1 = ((f32[32,1,2,128,256]{4,3,2,1,0:T(8,128)}), f32[32,1,2,128,256]{4,3,2,1,0:T(8,128)}, u32[]{:S(2)}, u32[]{:S(2)}) async-start(f32[32,1,2,128,256]{4,3,2,1,0:T(8,128)} %bitcast.89), calls=%async_computation.1 | async-start | bytes 16777216 | tf_op jit(solution)/shard_map/all_to_all | solution.py:74
  39.3 11.1 %copy-start.3 = (f32[2,3,31]{2,0,1:T(2,128)S(1)}, f32[2,3,31]{2,0,1:T(2,128)}, u32[]{:S(2)}) copy-start(f32[2,3,31]{2,0,1:T(2,128)} %param.14) | copy-start | bytes 2236
  39.3 308.6 %all-reduce.3.cloned.1.call-start = ((), (), s32[]{:S(2)}) async-start(), calls=%async_computation.2 | async-start | bytes 4194304 | tf_op jit(solution)/shard_map/psum | solution.py:121
  41.7 9.7 %copy-start.4 = (s32[2,2]{1,0:T(2,128)S(1)}, s32[2,2]{1,0:T(2,128)}, u32[]{:S(2)}) copy-start(s32[2,2]{1,0:T(2,128)} %param.12) | copy-start | bytes 52
  41.7 10.4 %copy-start.5 = (f32[2]{0:T(128)S(1)}, f32[2]{0:T(128)}, u32[]{:S(2)}) copy-start(f32[2]{0:T(128)} %param.15) | copy-start | bytes 28
  41.7 113.5 %collective-permute-start = (f32[15,128,256]{2,1,0:T(8,128)}, f32[15,128,256]{2,1,0:T(8,128)}, u32[]{:S(2)}, u32[]{:S(2)}) collective-permute-start(f32[15,128,256]{2,1,0:T(8,128)} %get-tuple-element.13), channel_id=1, source_target_pairs={{0,1},{1,2},{2,3},{3,4},{4,5},{5,6},{6,7},{7,8},{8,9},{9,10},{10,1... | collective-permute-start | bytes 5898248 | tf_op jit(solution)/shard_map/ppermute | solution.py:17
  45.4 114.3 %collective-permute-start.1 = (f32[15,128,256]{2,1,0:T(8,128)}, f32[15,128,256]{2,1,0:T(8,128)}, u32[]{:S(2)}, u32[]{:S(2)}) collective-permute-start(f32[15,128,256]{2,1,0:T(8,128)} %get-tuple-element.14), channel_id=1, source_target_pairs={{1,0},{2,1},{3,2},{4,3},{5,4},{6,5},{7,6},{8,7},{9,8},{10,9},{11,1... | collective-permute-start | bytes 5898248 | tf_op jit(solution)/shard_map/ppermute | solution.py:19
  54.2 108.2 %copy-start.2 = (f32[16,128,256]{2,0,1:T(8,128)S(1)}, f32[16,128,256]{2,0,1:T(8,128)}, u32[]{:S(2)}) copy-start(f32[16,128,256]{2,0,1:T(8,128)} %copy.103) | copy-start | bytes 6291460
  215.7 44.6 %collective-permute-start.2 = (f32[2,15,128,256]{3,2,1,0:T(8,128)S(1)}, f32[2,15,128,256]{3,2,1,0:T(8,128)S(1)}, u32[]{:S(2)}, u32[]{:S(2)}) collective-permute-start(f32[2,15,128,256]{3,2,1,0:T(8,128)S(1)} %get-tuple-element.9), channel_id=1, source_target_pairs={{0,1},{1,2},{2,3},{3,4},{4,5},{5,6},{6,7},{7,8},{8,9},{9,10},{10,1... | collective-permute-start | bytes 11796488 | tf_op jit(solution)/shard_map/ppermute | solution.py:17
  217.7 47.0 %collective-permute-start.3 = (f32[2,15,128,256]{3,2,1,0:T(8,128)S(1)}, f32[2,15,128,256]{3,2,1,0:T(8,128)S(1)}, u32[]{:S(2)}, u32[]{:S(2)}) collective-permute-start(f32[2,15,128,256]{3,2,1,0:T(8,128)S(1)} %get-tuple-element.10), channel_id=1, source_target_pairs={{1,0},{2,1},{3,2},{4,3},{5,4},{6,5},{7,6},{8,7},{9,8},{10,9},{11,1... | collective-permute-start | bytes 11796488 | tf_op jit(solution)/shard_map/ppermute | solution.py:19
  267.5 13.3 %copy-start.6 = (s32[8]{0:T(128)S(1)}, s32[8]{0:T(128)}, u32[]{:S(2)}) copy-start(s32[8]{0:T(128)} %param.13) | copy-start | bytes 100
  280.7 255.0 %all-reduce.5.cloned.1.call-start = ((), (), s32[]{:S(2)}) async-start(), calls=%async_computation.3 | async-start | bytes 4194304 | tf_op jit(solution)/shard_map/psum | solution.py:121
  353.2 25.4 %collective-permute-start.4 = (f32[15,128,256]{2,1,0:T(8,128)S(1)}, f32[15,128,256]{2,1,0:T(8,128)S(1)}, u32[]{:S(2)}, u32[]{:S(2)}) collective-permute-start(f32[15,128,256]{2,1,0:T(8,128)S(1)} %copy.104), channel_id=1, source_target_pairs={{0,1},{1,2},{2,3},{3,4},{4,5},{5,6},{6,7},{7,8},{8,9},{9,10},{10,1... | collective-permute-start | bytes 5898248 | tf_op jit(solution)/shard_map/ppermute | solution.py:17
  358.2 25.9 %collective-permute-start.5 = (f32[15,128,256]{2,1,0:T(8,128)S(1)}, f32[15,128,256]{2,1,0:T(8,128)S(1)}, u32[]{:S(2)}, u32[]{:S(2)}) collective-permute-start(f32[15,128,256]{2,1,0:T(8,128)S(1)} %copy.105), channel_id=1, source_target_pairs={{1,0},{2,1},{3,2},{4,3},{5,4},{6,5},{7,6},{8,7},{9,8},{10,9},{11,1... | collective-permute-start | bytes 5898248 | tf_op jit(solution)/shard_map/ppermute | solution.py:19
  396.3 3.7 copy-start
  409.4 44.5 %collective-permute-start.6 = (f32[2,15,128,256]{3,2,1,0:T(8,128)S(1)}, f32[2,15,128,256]{3,2,1,0:T(8,128)S(1)}, u32[]{:S(2)}, u32[]{:S(2)}) collective-permute-start(f32[2,15,128,256]{3,2,1,0:T(8,128)S(1)} %get-tuple-element.7), channel_id=1, source_target_pairs={{0,1},{1,2},{2,3},{3,4},{4,5},{5,6},{6,7},{7,8},{8,9},{9,10},{10,1... | collective-permute-start | bytes 11796488 | tf_op jit(solution)/shard_map/ppermute | solution.py:17
  411.3 47.0 %collective-permute-start.7 = (f32[2,15,128,256]{3,2,1,0:T(8,128)S(1)}, f32[2,15,128,256]{3,2,1,0:T(8,128)S(1)}, u32[]{:S(2)}, u32[]{:S(2)}) collective-permute-start(f32[2,15,128,256]{3,2,1,0:T(8,128)S(1)} %get-tuple-element.8), channel_id=1, source_target_pairs={{1,0},{2,1},{3,2},{4,3},{5,4},{6,5},{7,6},{8,7},{9,8},{10,9},{11,1... | collective-permute-start | bytes 11796488 | tf_op jit(solution)/shard_map/ppermute | solution.py:19
Sparse Core Ops, SparseCore 0:
  280.8 67.0 all-reduce.2
  474.2 61.4 all-reduce.4
where the time goes:
time: 551 us; the launch traced here: 548 us
  waiting for transfers between devices  342 us (62%)
  matrix products  89.7 us (16%)
  local copies, waits for them, and re-layouts  48.8 us (9%)
  starting transfers between devices  38.7 us (7%)
  other arithmetic  14.2 us (3%)
  between operations  14.2 us (3%)
    ppermute x4, waiting for transfers between devices, with_halo(): lax.ppermute(tail, axis, [(i, (i + 1) % count) for i in range(ends)])  198 us
    psum x2, waiting for transfers between devices, on_device(): summed = lax.psum(partial_logarithm, 'view')  129 us
    dot_general x2, matrix products, on_device(): corrected = jnp.einsum('vwyz,vwx->vxyz', rimmed, adj_x, precision=highest)  26.5 us
    dot_general x2, matrix products, on_device(): jnp.einsum('vxyz,vyq->vxqz', along_x, mat_y, precision=highest)  23.4 us
    ppermute x4, waiting for transfers between devices, with_halo(): lax.ppermute(head, axis, [((i + 1) % count, i) for i in range(ends)])  15 us
    scatter x1, local copies, waits for them, and re-layouts, on_device(): placed = jnp.zeros((per_group * per_block, planes, ny_cells, nz_cells), j...  13 us
    ppermute x4, starting transfers between devices, with_halo(): lax.ppermute(tail, axis, [(i, (i + 1) % count) for i in range(ends)])  11.4 us
  transfers between devices with their start and end apart: 12, of which 10 were waited for; matrix products, arithmetic and copies ran while one was open for 10% of the time, Pallas kernels for 0%

commit v1 on v0

--- a/solution.py
+++ b/solution.py
@@ -118,7 +118,13 @@
         rimmed = with_halo(back_y, (("block", 1),), reach)
         corrected = jnp.einsum("vwyz,vwx->vxyz", rimmed, adj_x, precision=highest)
         partial_logarithm = jnp.sum(live_cells * weights * jnp.log(corrected), axis=0)
-        summed = lax.psum(partial_logarithm, "view")
+        devices = lax.axis_size("view")
+        summed, far = (partial_logarithm, 1)
+        while far < devices:
+            summed = summed + lax.ppermute(
+                summed, "view", [(i_2, i_2 ^ far) for i_2 in range(devices)]
+            )
+            far = 2 * far
         current = current * jnp.exp(summed / counts)
     return current
 

time: 551 us -> 591 us (1.073)
  the two profiles are of different devices: /device:TPU:1 before, /device:TPU:5 now
where the time goes in v1:
time: 591 us; the launch traced here: 588 us
  waiting for transfers between devices  395 us (67%)
  matrix products  76 us (13%)
  starting transfers between devices  52.5 us (9%)
  local copies, waits for them, and re-layouts  49.2 us (8%)
  other arithmetic  14.9 us (3%)
    ppermute x4, waiting for transfers between devices, with_halo(): lax.ppermute(tail, axis, [(i, (i + 1) % count) for i in range(ends)])  204 us
    ppermute x4, waiting for transfers between devices, on_device(): lax.ppermute(summed, 'view', [(i_2, i_2 ^ far) for i_2 in range(devices)])  177 us
    dot_general x2, matrix products, on_device(): corrected = jnp.einsum('vwyz,vwx->vxyz', rimmed, adj_x, precision=highest)  23.9 us
    ppermute x4, starting transfers between devices, with_halo(): lax.ppermute(tail, axis, [(i, (i + 1) % count) for i in range(ends)])  17.8 us
    scatter x1, local copies, waits for them, and re-layouts, on_device(): placed = jnp.zeros((per_group * per_block, planes, ny_cells, nz_cells), j...  13.5 us
    ppermute x4, waiting for transfers between devices, with_halo(): lax.ppermute(head, axis, [((i + 1) % count, i) for i in range(ends)])  13.4 us
    dot_general x2, matrix products, on_device(): jnp.einsum('vxyz,vyq->vxqz', along_x, mat_y, precision=highest)  12.3 us
  transfers between devices with their start and end apart: 14, of which 11 were waited for; matrix products, arithmetic and copies ran while one was open for 8% of the time, Pallas kernels for 0%

profile of v1, /device:TPU:5, one launch (start us, length us, event | category | flops | bytes accessed | tf_op | source)
XLA Modules:
  0.0 587.9 jit_solution(7574191024826737545)
XLA Ops:
  3.6 8.7 %all-to-all-start = ((f32[32,1,1]{2,1,0:T(1,128)}), f32[32,1,1]{2,1,0:T(1,128)S(1)}, u32[]{:S(2)}, u32[]{:S(2)}) async-start(f32[32,1,1]{2,1,0:T(1,128)} %copy.91), calls=%async_computation | async-start | bytes 32768 | tf_op jit(solution)/shard_map/all_to_all | solution.py:81
  16.5 7.3 %scatter_fusion = f32[32,2,128,256]{3,2,1,0:T(8,128)} fusion(f32[32,2,128,256]{3,2,1,0:T(8,128)} %broadcast_in_dim.37, s32[16]{0:T(128)S(1)} %fusion.58, f32[16,2,128,256]{3,2,1,0:T(8,128)} %bitcast.92), kind=kCustom, calls=%fused_computation.1 | custom fusion | bytes 12582976 | tf_op jit(solution)/shard_map/scatter | solution.py:66
  23.8 8.2 %all-to-all-start.1 = ((f32[32,1,2,128,256]{4,3,2,1,0:T(8,128)}), f32[32,1,2,128,256]{4,3,2,1,0:T(8,128)}, u32[]{:S(2)}, u32[]{:S(2)}) async-start(f32[32,1,2,128,256]{4,3,2,1,0:T(8,128)} %bitcast.89), calls=%async_computation.1 | async-start | bytes 16777216 | tf_op jit(solution)/shard_map/all_to_all | solution.py:74
  47.0 104.9 %collective-permute-done = f32[15,128,256]{2,1,0:T(8,128)} collective-permute-done((f32[15,128,256]{2,1,0:T(8,128)}, f32[15,128,256]{2,1,0:T(8,128)}, u32[]{:S(2)}, u32[]{:S(2)}) %collective-permute-start) | collective-permute-done | bytes 1966112 | tf_op jit(solution)/shard_map/ppermute | solution.py:17
  157.3 4.7 fusion.5
  162.0 6.3 %fusion.29 = f32[2,128,16,256]{3,1,2,0:T(8,128)S(1)} fusion(f32[2,128,128,1]{1,2,3,0:T(8,128)S(1)} %copy.118, f32[2,16,128,256]{3,1,2,0:T(8,128)S(1)} %fusion.5), kind=kOutput, calls=%fused_computation.37 | convolution fusion | flops 1610612736 | bytes 8519680 | tf_op jit(solution)/shard_map/vxyz,vyq->vxqz/dot_general | solution.py:113
  168.2 4.9 fusion.17
  175.6 13.5 %scatter_fusion.1 = f32[16,2,128,256]{3,2,1,0:T(8,128)} fusion(f32[16,2,128,256]{3,2,1,0:T(8,128)} %broadcast_in_dim.33, s32[32]{0:T(128)S(1)} %fusion.57, f32[32,2,128,256]{3,2,1,0:T(8,128)} %bitcast.15), kind=kCustom, calls=%fused_computation.2 | custom fusion | bytes 25165952 | tf_op jit(solution)/shard_map/scatter | solution.py:90
  189.1 6.4 %fusion.21 = f32[2,16,128,256]{3,2,1,0:T(8,128)S(1)} fusion(f32[2,16,128,256]{3,2,1,0:T(8,128)} %fusion.17, f32[2,16]{1,0:T(2,128)S(1)} %get-tuple-element.16, f32[2,16]{1,0:T(2,128)S(1)} %broadcast_in_dim_reshape.4, f32[2,256,256,1]{2,0,1,3:T(2,128)S(1)} %fusion.41, f32[2,16,128,256]{3,2,1,0:T(8,128)} %bitcast.90), kind=kOutput, calls=%fused_computation.31 | convolution fusion | flops 3224371200 | bytes 13107456 | tf_op jit(solution)/shard_map/vxyz,vqz->vxyq/dot_general | solution.py:116
  200.2 4.4 collective-permute-start.2
  206.8 40.5 %collective-permute-done.2 = f32[2,15,128,256]{3,2,1,0:T(8,128)S(1)} collective-permute-done((f32[2,15,128,256]{3,2,1,0:T(8,128)S(1)}, f32[2,15,128,256]{3,2,1,0:T(8,128)S(1)}, u32[]{:S(2)}, u32[]{:S(2)}) %collective-permute-start.2) | collective-permute-done | bytes 3932192 | tf_op jit(solution)/shard_map/ppermute | solution.py:17
  254.1 12.0 %multiply_reduce_fusion.1 = f32[16,128,256]{2,0,1:T(8,128)S(1)} fusion(f32[2,46,128,256]{3,2,1,0:T(8,128)S(1)} %pad_maximum_fusion, f32[2,16]{1,0:T(2,128)S(1)} %get-tuple-element.15, f32[2,46,16,1]{1,0,2,3:T(2,128)S(1)} %convolution_bitcast_fusion.3), kind=kOutput, calls=%fused_computation.40 | convolution fusion | flops 580386816 | bytes 14161792 | tf_op jit(solution)/shard_map/vwyz,vwx->vxyz/dot_general | solution.py:119
  268.3 42.3 %collective-permute-done.4 = f32[16,128,256]{2,0,1:T(8,128)S(1)} collective-permute-done((f32[16,128,256]{2,0,1:T(8,128)S(1)}, f32[16,128,256]{2,0,1:T(8,128)S(1)}, u32[]{:S(2)}, u32[]{:S(2)}) %collective-permute-start.4) | collective-permute-done | bytes 2097184 | tf_op jit(solution)/shard_map/ppermute | solution.py:124
  315.5 43.6 %collective-permute-done.5 = f32[16,128,256]{2,0,1:T(8,128)} collective-permute-done((f32[16,128,256]{2,0,1:T(8,128)}, f32[16,128,256]{2,0,1:T(8,128)}, u32[]{:S(2)}, u32[]{:S(2)}) %collective-permute-start.5) | collective-permute-done | bytes 2097184 | tf_op jit(solution)/shard_map/ppermute | solution.py:124
  364.6 8.2 %collective-permute-start.6 = (f32[15,128,256]{2,1,0:T(8,128)S(1)}, f32[15,128,256]{2,1,0:T(8,128)S(1)}, u32[]{:S(2)}, u32[]{:S(2)}) collective-permute-start(f32[15,128,256]{2,1,0:T(8,128)S(1)} %copy.104), channel_id=1, source_target_pairs={{0,1},{1,2},{2,3},{3,4},{4,5},{5,6},{6,7},{7,8},{8,9},{9,10},{10,1... | collective-permute-start | bytes 5898248 | tf_op jit(solution)/shard_map/ppermute | solution.py:17
  376.3 18.1 %collective-permute-done.6 = f32[15,128,256]{2,1,0:T(8,128)S(1)} collective-permute-done((f32[15,128,256]{2,1,0:T(8,128)S(1)}, f32[15,128,256]{2,1,0:T(8,128)S(1)}, u32[]{:S(2)}, u32[]{:S(2)}) %collective-permute-start.6) | collective-permute-done | bytes 1966112 | tf_op jit(solution)/shard_map/ppermute | solution.py:17
  401.1 4.7 fusion.10
  405.8 6.1 %fusion.27 = f32[2,128,16,256]{3,1,2,0:T(8,128)S(1)} fusion(f32[2,128,128,1]{1,2,3,0:T(8,128)S(1)} %copy.118, f32[2,16,128,256]{3,1,2,0:T(8,128)S(1)} %fusion.10), kind=kOutput, calls=%fused_computation.35 | convolution fusion | flops 1610612736 | bytes 8519680 | tf_op jit(solution)/shard_map/vxyz,vyq->vxqz/dot_general | solution.py:113
  415.6 4.4 fusion.25
  429.3 40.2 %collective-permute-done.8 = f32[2,15,128,256]{3,2,1,0:T(8,128)S(1)} collective-permute-done((f32[2,15,128,256]{3,2,1,0:T(8,128)S(1)}, f32[2,15,128,256]{3,2,1,0:T(8,128)S(1)}, u32[]{:S(2)}, u32[]{:S(2)}) %collective-permute-start.8) | collective-permute-done | bytes 3932192 | tf_op jit(solution)/shard_map/ppermute | solution.py:17
  469.5 4.6 collective-permute-done.9
  476.4 11.9 %multiply_reduce_fusion = f32[16,128,256]{2,0,1:T(8,128)S(1)} fusion(f32[2,46,128,256]{3,2,1,0:T(8,128)S(1)} %pad_maximum_fusion.1, f32[2,16]{1,0:T(2,128)S(1)} %get-tuple-element.15, f32[2,46,16,1]{1,0,2,3:T(2,128)S(1)} %convolution_bitcast_fusion.3), kind=kOutput, calls=%fused_computation.39 | convolution fusion | flops 580386816 | bytes 14161792 | tf_op jit(solution)/shard_map/vwyz,vwx->vxyz/dot_general | solution.py:119
  489.6 44.9 %collective-permute-done.10 = f32[16,128,256]{2,0,1:T(8,128)S(1)} collective-permute-done((f32[16,128,256]{2,0,1:T(8,128)S(1)}, f32[16,128,256]{2,0,1:T(8,128)S(1)}, u32[]{:S(2)}, u32[]{:S(2)}) %collective-permute-start.10) | collective-permute-done | bytes 2097184 | tf_op jit(solution)/shard_map/ppermute | solution.py:124
  537.7 46.6 %collective-permute-done.11 = f32[16,128,256]{2,0,1:T(8,128)S(1)} collective-permute-done((f32[16,128,256]{2,0,1:T(8,128)S(1)}, f32[16,128,256]{2,0,1:T(8,128)S(1)}, u32[]{:S(2)}, u32[]{:S(2)}) %collective-permute-start.11) | collective-permute-done | bytes 2097184 | tf_op jit(solution)/shard_map/ppermute | solution.py:124
  (75 shorter events, 89.8 us)
Async XLA Ops:
  3.6 20.3 %all-to-all-start = ((f32[32,1,1]{2,1,0:T(1,128)}), f32[32,1,1]{2,1,0:T(1,128)S(1)}, u32[]{:S(2)}, u32[]{:S(2)}) async-start(f32[32,1,1]{2,1,0:T(1,128)} %copy.91), calls=%async_computation | async-start | bytes 32768 | tf_op jit(solution)/shard_map/all_to_all | solution.py:81
  23.8 8.2 %copy-start.1 = (f32[16,128,256]{2,1,0:T(8,128)S(1)}, f32[16,128,256]{2,1,0:T(8,128)}, u32[]{:S(2)}) copy-start(f32[16,128,256]{2,1,0:T(8,128)} %param.8) | copy-start | bytes 6291460
  23.8 149.3 %all-to-all-start.1 = ((f32[32,1,2,128,256]{4,3,2,1,0:T(8,128)}), f32[32,1,2,128,256]{4,3,2,1,0:T(8,128)}, u32[]{:S(2)}, u32[]{:S(2)}) async-start(f32[32,1,2,128,256]{4,3,2,1,0:T(8,128)} %bitcast.89), calls=%async_computation.1 | async-start | bytes 16777216 | tf_op jit(solution)/shard_map/all_to_all | solution.py:74
  32.1 10.3 %copy-start.3 = (f32[2,3,31]{2,0,1:T(2,128)S(1)}, f32[2,3,31]{2,0,1:T(2,128)}, u32[]{:S(2)}) copy-start(f32[2,3,31]{2,0,1:T(2,128)} %param.14) | copy-start | bytes 2236
  34.6 8.9 %copy-start.4 = (s32[2,2]{1,0:T(2,128)S(1)}, s32[2,2]{1,0:T(2,128)}, u32[]{:S(2)}) copy-start(s32[2,2]{1,0:T(2,128)} %param.12) | copy-start | bytes 52
  34.6 9.6 %copy-start.5 = (f32[2]{0:T(128)S(1)}, f32[2]{0:T(128)}, u32[]{:S(2)}) copy-start(f32[2]{0:T(128)} %param.15) | copy-start | bytes 28
  34.6 117.3 %collective-permute-start = (f32[15,128,256]{2,1,0:T(8,128)}, f32[15,128,256]{2,1,0:T(8,128)}, u32[]{:S(2)}, u32[]{:S(2)}) collective-permute-start(f32[15,128,256]{2,1,0:T(8,128)} %get-tuple-element.13), channel_id=1, source_target_pairs={{0,1},{1,2},{2,3},{3,4},{4,5},{5,6},{6,7},{7,8},{8,9},{9,10},{10,1... | collective-permute-start | bytes 5898248 | tf_op jit(solution)/shard_map/ppermute | solution.py:17
  37.8 116.8 %collective-permute-start.1 = (f32[15,128,256]{2,1,0:T(8,128)}, f32[15,128,256]{2,1,0:T(8,128)}, u32[]{:S(2)}, u32[]{:S(2)}) collective-permute-start(f32[15,128,256]{2,1,0:T(8,128)} %get-tuple-element.14), channel_id=1, source_target_pairs={{1,0},{2,1},{3,2},{4,3},{5,4},{6,5},{7,6},{8,7},{9,8},{10,9},{11,1... | collective-permute-start | bytes 5898248 | tf_op jit(solution)/shard_map/ppermute | solution.py:19
  46.3 111.0 %copy-start.2 = (f32[16,128,256]{2,0,1:T(8,128)S(1)}, f32[16,128,256]{2,0,1:T(8,128)}, u32[]{:S(2)}) copy-start(f32[16,128,256]{2,0,1:T(8,128)} %copy.103) | copy-start | bytes 6291460
  200.2 47.0 %collective-permute-start.2 = (f32[2,15,128,256]{3,2,1,0:T(8,128)S(1)}, f32[2,15,128,256]{3,2,1,0:T(8,128)S(1)}, u32[]{:S(2)}, u32[]{:S(2)}) collective-permute-start(f32[2,15,128,256]{3,2,1,0:T(8,128)S(1)} %get-tuple-element.9), channel_id=1, source_target_pairs={{0,1},{1,2},{2,3},{3,4},{4,5},{5,6},{6,7},{7,8},{8,9},{9,10},{10,1... | collective-permute-start | bytes 11796488 | tf_op jit(solution)/shard_map/ppermute | solution.py:17
  204.6 47.0 %collective-permute-start.3 = (f32[2,15,128,256]{3,2,1,0:T(8,128)S(1)}, f32[2,15,128,256]{3,2,1,0:T(8,128)S(1)}, u32[]{:S(2)}, u32[]{:S(2)}) collective-permute-start(f32[2,15,128,256]{3,2,1,0:T(8,128)S(1)} %get-tuple-element.10), channel_id=1, source_target_pairs={{1,0},{2,1},{3,2},{4,3},{5,4},{6,5},{7,6},{8,7},{9,8},{10,9},{11,1... | collective-permute-start | bytes 11796488 | tf_op jit(solution)/shard_map/ppermute | solution.py:19
  266.1 49.3 %copy-start.6 = (s32[8]{0:T(128)S(1)}, s32[8]{0:T(128)}, u32[]{:S(2)}) copy-start(s32[8]{0:T(128)} %param.13) | copy-start | bytes 100
  266.1 44.5 %collective-permute-start.4 = (f32[16,128,256]{2,0,1:T(8,128)S(1)}, f32[16,128,256]{2,0,1:T(8,128)S(1)}, u32[]{:S(2)}, u32[]{:S(2)}) collective-permute-start(f32[16,128,256]{2,0,1:T(8,128)S(1)} %multiply_reduce_fusion.1), channel_id=1, source_target_pairs={{0,32},{32,0},{64,96},{96,64},{1,33},{33,1},{65,97},{97,65},{2,34}... | collective-permute-start | bytes 6291464 | tf_op jit(solution)/shard_map/ppermute | solution.py:124
  312.4 46.7 %collective-permute-start.5 = (f32[16,128,256]{2,0,1:T(8,128)}, f32[16,128,256]{2,0,1:T(8,128)}, u32[]{:S(2)}, u32[]{:S(2)}) collective-permute-start(f32[16,128,256]{2,0,1:T(8,128)} %add.103), channel_id=1, source_target_pairs={{0,64},{32,96},{64,0},{96,32},{1,65},{33,97},{65,1},{97,33},{2,66}... | collective-permute-start | bytes 6291464 | tf_op jit(solution)/shard_map/ppermute | solution.py:124
  364.6 29.8 %collective-permute-start.6 = (f32[15,128,256]{2,1,0:T(8,128)S(1)}, f32[15,128,256]{2,1,0:T(8,128)S(1)}, u32[]{:S(2)}, u32[]{:S(2)}) collective-permute-start(f32[15,128,256]{2,1,0:T(8,128)S(1)} %copy.104), channel_id=1, source_target_pairs={{0,1},{1,2},{2,3},{3,4},{4,5},{5,6},{6,7},{7,8},{8,9},{9,10},{10,1... | collective-permute-start | bytes 5898248 | tf_op jit(solution)/shard_map/ppermute | solution.py:17
  374.0 25.9 %collective-permute-start.7 = (f32[15,128,256]{2,1,0:T(8,128)S(1)}, f32[15,128,256]{2,1,0:T(8,128)S(1)}, u32[]{:S(2)}, u32[]{:S(2)}) collective-permute-start(f32[15,128,256]{2,1,0:T(8,128)S(1)} %copy.105), channel_id=1, source_target_pairs={{1,0},{2,1},{3,2},{4,3},{5,4},{6,5},{7,6},{8,7},{9,8},{10,9},{11,1... | collective-permute-start | bytes 5898248 | tf_op jit(solution)/shard_map/ppermute | solution.py:19
  411.9 3.7 copy-start
  424.9 44.5 %collective-permute-start.8 = (f32[2,15,128,256]{3,2,1,0:T(8,128)S(1)}, f32[2,15,128,256]{3,2,1,0:T(8,128)S(1)}, u32[]{:S(2)}, u32[]{:S(2)}) collective-permute-start(f32[2,15,128,256]{3,2,1,0:T(8,128)S(1)} %get-tuple-element.7), channel_id=1, source_target_pairs={{0,1},{1,2},{2,3},{3,4},{4,5},{5,6},{6,7},{7,8},{8,9},{9,10},{10,1... | collective-permute-start | bytes 11796488 | tf_op jit(solution)/shard_map/ppermute | solution.py:17
  426.9 47.2 %collective-permute-start.9 = (f32[2,15,128,256]{3,2,1,0:T(8,128)S(1)}, f32[2,15,128,256]{3,2,1,0:T(8,128)S(1)}, u32[]{:S(2)}, u32[]{:S(2)}) collective-permute-start(f32[2,15,128,256]{3,2,1,0:T(8,128)S(1)} %get-tuple-element.8), channel_id=1, source_target_pairs={{1,0},{2,1},{3,2},{4,3},{5,4},{6,5},{7,6},{8,7},{9,8},{10,9},{11,1... | collective-permute-start | bytes 11796488 | tf_op jit(solution)/shard_map/ppermute | solution.py:19
  488.3 46.3 %collective-permute-start.10 = (f32[16,128,256]{2,0,1:T(8,128)S(1)}, f32[16,128,256]{2,0,1:T(8,128)S(1)}, u32[]{:S(2)}, u32[]{:S(2)}) collective-permute-start(f32[16,128,256]{2,0,1:T(8,128)S(1)} %multiply_reduce_fusion), channel_id=1, source_target_pairs={{0,32},{32,0},{64,96},{96,64},{1,33},{33,1},{65,97},{97,65},{2,34}... | collective-permute-start | bytes 6291464 | tf_op jit(solution)/shard_map/ppermute | solution.py:124
  535.1 49.2 %collective-permute-start.11 = (f32[16,128,256]{2,0,1:T(8,128)S(1)}, f32[16,128,256]{2,0,1:T(8,128)S(1)}, u32[]{:S(2)}, u32[]{:S(2)}) collective-permute-start(f32[16,128,256]{2,0,1:T(8,128)S(1)} %add.106), channel_id=1, source_target_pairs={{0,64},{32,96},{64,0},{96,32},{1,65},{33,97},{65,1},{97,33},{2,66}... | collective-permute-start | bytes 6291464 | tf_op jit(solution)/shard_map/ppermute | solution.py:124
